TPU v7x, 32 devices: a whole 2x2x4 slice. The times are simulated.
32 devices in a mesh: grp: 2 (over x), smp: 16 (over z, y, core).
Axes of the slice: x: 2, y: 2, z: 4, core: 2. Of those that a mesh axis runs over, the one named last changes fastest.
Arguments:
- state: bfloat16 [512, 16, 1024], P(('grp', 'smp')), parts along dimension 0, may hold values from -40 to 40
- unit_slot: int32 [512, 64], P(('grp', 'smp')), parts along dimension 0, may hold values from 0 to 511
- token_count: int32 [512], P(('grp', 'smp')), parts along dimension 0, may hold values from 48 to 64, as said below
- session: int32 [512], P(('grp', 'smp')), parts along dimension 0, may hold values from 0 to 15, as said below
- session_row: int32 [32], P('grp'), parts along dimension 0, may hold values from 0 to 15, as said below
- unit_count: int32 [16], replicated, may hold values from 128 to 512, as said below
- panels: bfloat16 [16, 512, 1024], P('smp'), may hold values from -40 to 40
- memory_key: bfloat16 [512, 1024], P(('grp', 'smp')), parts along dimension 0, may hold values from -240 to 240
- memory_value: bfloat16 [512, 1024], P(('grp', 'smp')), parts along dimension 0, may hold values from -24 to 24
- q1_weight: bfloat16 [1024, 1024], replicated, may hold values from -0.1875 to 0.1875
- o1_weight: bfloat16 [1024, 1024], replicated, may hold values from -0.1875 to 0.1875
- kv_weight: bfloat16 [1024, 2048], replicated, may hold values from -6 to 6
- q2_weight: bfloat16 [1024, 1024], replicated, may hold values from -0.1875 to 0.1875
- o2_weight: bfloat16 [1024, 1024], replicated, may hold values from -0.1875 to 0.1875
Outputs:
- latent_out: bfloat16 [512, 16, 1024], P(('grp', 'smp')), parts along dimension 0
There are 2 independent parts, one for each index of `grp`. A program takes and returns all parts, laid end to end along the dimension named above; an argument that names none is the same for every part. Nothing has to cross between parts.
Inputs may be any that keep to these rules, and one draw needn't show every extreme that they name: The panel row of session s is session_row[s]; it lies on the device of index session_row[s]. session_row is a permutation. The 16 samples of one device have sessions on 16 different devices; one device holds the session of one sample on every device. `token_count`: some sample on every device has 64 tokens. `unit_count`: some panel row has 512 units.
All inputs are finite; a program needn't handle non-finite values.
Results may differ from a plain program's by a relative error of at most 0.007.
The roundings to bfloat16 on the way count: a program that leaves them out, or rounds other values in their place, can miss the bound.
Values may be sent and summed in bfloat16 or wider, within the bound.
No kernel may reach another device: no remote copies, remote signals or barrier semaphores. Data moves between devices by JAX's collectives and lax.ppermute only.
A program may use at most 128 MiB of HBM per device.

v0:
```python
import jax
import jax.numpy as jnp
from jax import lax
from jax.sharding import PartitionSpec as P

HEAD_DIM = 64
masked_score = -1e30


def normed(values):
    wide = values.astype(jnp.float32)
    return (wide * lax.rsqrt(jnp.mean(wide * wide, axis=-1, keepdims=True) + 1e-05)).astype(
        jnp.bfloat16
    )


def attend(queries, key_rows, value_rows, live_tokens):
    samples, latents, head_count, head_size = queries.shape
    spike_scores = jnp.einsum(
        "blhd,bkhd->bhlk", queries, key_rows, preferred_element_type=jnp.float32
    ) * HEAD_DIM ** (-0.5)
    spike_scores = jnp.where(live_tokens[:, None, None, :], spike_scores, masked_score)
    spike_max = jnp.max(spike_scores, axis=-1, keepdims=True)
    spike_exp = jnp.exp(spike_scores - spike_max)
    denominator = jnp.transpose(jnp.sum(spike_exp, axis=-1, keepdims=True), (0, 2, 1, 3))
    spike_mix = (
        jnp.einsum(
            "bhlk,bkhd->blhd",
            spike_exp.astype(jnp.bfloat16),
            value_rows,
            preferred_element_type=jnp.float32,
        )
        / denominator
    )
    return spike_mix.reshape(samples, latents, head_count * head_size).astype(jnp.bfloat16)


def per_device(
    state,
    unit_slot,
    token_count,
    session,
    session_row,
    unit_count,
    panels,
    memory_key,
    memory_value,
    q1_weight,
    o1_weight,
    kv_weight,
    q2_weight,
    o2_weight,
):
    local_samples, latents, model_width = state.shape
    token_total = unit_slot.shape[1]
    owners = lax.axis_size("smp")
    sess_dev, unit_total = (panels.shape[0], panels.shape[1])
    head_count = model_width // HEAD_DIM
    session_ids = jnp.arange(session_row.shape[0], dtype=jnp.int32)
    panel_row = jnp.sum(
        jnp.where(session[:, None] == session_ids[None, :], session_row[None, :], 0), axis=1
    )
    unit_limit = jnp.sum(
        jnp.where(panel_row[:, None] == session_ids[None, :], unit_count[None, :], 0), axis=1
    )
    owner_rank = panel_row // sess_dev
    token_index = (panel_row % sess_dev * unit_total)[:, None] + unit_slot % unit_limit[:, None]
    slot_pick = owner_rank[None, :] == jnp.arange(owners, dtype=jnp.int32)[:, None]
    request = jnp.sum(jnp.where(slot_pick[:, :, None], token_index[None, :, :], 0), axis=1)
    live_tokens = jnp.arange(token_total, dtype=jnp.int32)[None, :] < token_count[:, None]
    panel_table = panels.reshape(sess_dev * unit_total, model_width)
    arrived = lax.all_to_all(
        panel_table[lax.all_to_all(request, "smp", split_axis=0, concat_axis=0, tiled=True)],
        "smp",
        split_axis=0,
        concat_axis=0,
        tiled=True,
    )
    row_total = local_samples * latents
    flat_state = state.reshape(row_total, model_width)
    queries = jnp.dot(normed(flat_state), q1_weight, preferred_element_type=jnp.float32).astype(
        jnp.bfloat16
    )
    queries = queries.reshape(row_total, head_count, HEAD_DIM)
    running_max = jnp.full((head_count, row_total), masked_score, jnp.float32)
    key_rows = lax.all_gather(memory_key, "smp", axis=0, tiled=True).reshape(
        -1, head_count, HEAD_DIM
    )
    value_rows = lax.all_gather(memory_value, "smp", axis=0, tiled=True).reshape(
        -1, head_count, HEAD_DIM
    )
    scores = jnp.einsum(
        "rhd,khd->hrk", queries, key_rows, preferred_element_type=jnp.float32
    ) * HEAD_DIM ** (-0.5)
    new_max = jnp.maximum(running_max, jnp.max(scores, axis=-1))
    exponent = jnp.exp(scores - new_max[:, :, None])
    denominator = jnp.sum(exponent, axis=-1)
    weighted = jnp.einsum(
        "hrk,khd->hrd",
        exponent.astype(jnp.bfloat16),
        value_rows,
        preferred_element_type=jnp.float32,
    )
    running_max, denominator, weighted = (new_max, denominator, weighted)
    read_mem = (
        jnp.transpose(weighted / denominator[:, :, None], (1, 0, 2))
        .reshape(row_total, model_width)
        .astype(jnp.bfloat16)
    )
    hidden = (
        flat_state.astype(jnp.float32)
        + jnp.dot(read_mem, o1_weight, preferred_element_type=jnp.float32)
    ).astype(jnp.bfloat16)
    queries2 = jnp.dot(normed(hidden), q2_weight, preferred_element_type=jnp.float32).astype(
        jnp.bfloat16
    )
    queries2 = queries2.reshape(local_samples, latents, model_width)
    embed = arrived[owner_rank]
    key_value = jnp.dot(
        normed(embed.reshape(local_samples * token_total, model_width)),
        kv_weight,
        preferred_element_type=jnp.float32,
    ).astype(jnp.bfloat16)
    key_value = key_value.reshape(local_samples, token_total, 2 * model_width)
    key_rows = key_value[:, :, :model_width].reshape(
        local_samples, token_total, head_count, HEAD_DIM
    )
    value_rows = key_value[:, :, model_width:].reshape(
        local_samples, token_total, head_count, HEAD_DIM
    )
    read_spike = attend(
        queries2.reshape(local_samples, latents, head_count, HEAD_DIM),
        key_rows,
        value_rows,
        live_tokens,
    )
    result = hidden.astype(jnp.float32) + jnp.dot(
        read_spike.reshape(row_total, model_width), o2_weight, preferred_element_type=jnp.float32
    )
    return result.astype(jnp.bfloat16).reshape(local_samples, latents, model_width)


def solution(mesh):
    in_specs = (
        P(("grp", "smp"), None, None),
        P(("grp", "smp"), None),
        P(("grp", "smp")),
        P(("grp", "smp")),
        P("grp"),
        P(),
        P("smp", None, None),
        P(("grp", "smp"), None),
        P(("grp", "smp"), None),
        P(),
        P(),
        P(),
        P(),
        P(),
    )
    out_specs = P(("grp", "smp"), None, None)
    return jax.shard_map(
        per_device, mesh=mesh, in_specs=in_specs, out_specs=out_specs, check_vma=False
    )
```

profile of v0, /device:TPU:0, one launch (start us, length us, event | category | flops | bytes accessed | tf_op | source)
XLA Modules:
  0.0 167.4 jit_solution(13503824719128611106)
XLA Ops:
  0.0 1.0 select_reduce_fusion.2
  1.0 0.8 select_reduce_fusion.1
  1.9 0.9 add_select_fusion
  3.5 7.4 %all-to-all-start = ((s32[16,1,64]{2,1,0:T(1,128)}), s32[16,1,64]{2,1,0:T(1,128)S(1)}, u32[]{:S(2)}, u32[]{:S(2)}) async-start(s32[16,1,64]{2,1,0:T(1,128)} %bitcast.9), calls=%async_computation | async-start | bytes 16384 | tf_op jit(solution)/shard_map/all_to_all | solution.py:73
  10.9 1.2 multiply_reduce_fusion.2
  12.1 5.1 %all-to-all-done = s32[16,1,64]{2,1,0:T(1,128)S(1)} async-done(((s32[16,1,64]{2,1,0:T(1,128)}), s32[16,1,64]{2,1,0:T(1,128)S(1)}, u32[]{:S(2)}, u32[]{:S(2)}) %all-to-all-start) | async-done | bytes 4128 | tf_op jit(solution)/shard_map/all_to_all | solution.py:73
  17.3 7.4 %gather_fusion = bf16[1024,1024]{1,0:T(8,128)(2,1)} fusion(bf16[512,1024]{1,0:T(8,128)(2,1)} %bitcast.57, s32[1024]{0:T(1024)S(1)} %broadcast_clamp_fusion), kind=kCustom, calls=%fused_computation | custom fusion | bytes 4198400 | tf_op jit(solution)/shard_map/gather | solution.py:73
  24.7 4.6 %all-to-all-start.1 = ((bf16[16,64,1024]{2,1,0:T(8,128)(2,1)}), bf16[16,64,1024]{2,1,0:T(8,128)(2,1)}, u32[]{:S(2)}, u32[]{:S(2)}) async-start(bf16[16,64,1024]{2,1,0:T(8,128)(2,1)} %bitcast.58), calls=%async_computation.1 | async-start | bytes 4194304 | tf_op jit(solution)/shard_map/all_to_all | solution.py:72
  29.6 3.1 %convolution_convert_fusion.2 = bf16[256,1024]{1,0:T(8,128)(2,1)} fusion(bf16[256,1024]{1,0:T(8,128)(2,1)S(1)} %fusion.31, bf16[1024,1024]{1,0:T(8,128)(2,1)} %param.23), kind=kOutput, calls=%fused_computation.31 | convolution fusion | flops 537133056 | bytes 3145728 | tf_op jit(solution)/shard_map/dot_general | solution.py:81
  32.7 1.2 copy.36
  33.9 52.9 %all_gather.6 = bf16[256,1024]{1,0:T(8,128)(2,1)} all-gather(bf16[16,1024]{1,0:T(8,128)(2,1)S(1)} %copy-done.5), channel_id=1, replica_groups=mesh['grp'=2,'smp'=16] {'smp'}, dimensions={0}, use_global_device_ids=true | all-gather | bytes 557056 | tf_op jit(solution)/shard_map/all_gather | solution.py:86
  86.8 2.0 %copy.37 = bf16[256,1024]{0,1:T(8,128)(2,1)} copy(bf16[256,1024]{1,0:T(8,128)(2,1)} %all_gather.6) | data formatting | bytes 1048576 | tf_op jit(solution)/shard_map/all_gather | solution.py:86
  88.9 25.8 %all_gather.7 = bf16[256,1024]{1,0:T(8,128)(2,1)} all-gather(bf16[16,1024]{1,0:T(8,128)(2,1)S(1)} %copy-done.6), channel_id=1, replica_groups=mesh['grp'=2,'smp'=16] {'smp'}, dimensions={0}, use_global_device_ids=true | all-gather | bytes 557056 | tf_op jit(solution)/shard_map/all_gather | solution.py:89
  114.7 2.0 %copy.38 = bf16[256,1024]{0,1:T(8,128)(2,1)} copy(bf16[256,1024]{1,0:T(8,128)(2,1)} %all_gather.7) | data formatting | bytes 1048576 | tf_op jit(solution)/shard_map/all_gather | solution.py:89
  116.8 1.8 %multiply_reduce_fusion.1 = (f32[16,256]{1,0:T(8,128)S(1)}, f32[16,256,256]{1,2,0:T(8,128)S(1)}) fusion(bf16[256,16,64]{0,2,1:T(8,128)(2,1)S(1)} %bitcast.61, bf16[256,16,64]{0,2,1:T(8,128)(2,1)} %bitcast.62), kind=kOutput, calls=%fused_computation.10 | convolution fusion | flops 136310784 | bytes 5259264 | tf_op jit(solution)/shard_map/rhd,khd->hrk/dot_general | solution.py:92
  119.6 0.9 fusion.25
  120.5 0.8 fusion.28
  121.4 0.8 copy-done.4
  122.2 1.6 convolution_convert_fusion.1
  123.8 1.8 %reshape_reshape.3 = bf16[16,16,16,64]{3,2,1,0:T(8,128)(2,1)S(1)} reshape(bf16[256,1024]{1,0:T(8,128)(2,1)} %convolution_convert_fusion.1) | data formatting | bytes 1048576 | tf_op jit(solution)/shard_map/reshape;reshape | solution.py:132
  125.6 3.6 %gather_fusion.1 = bf16[16,64,1024]{2,1,0:T(8,128)(2,1)} fusion(bf16[16,64,1024]{2,1,0:T(8,128)(2,1)} %all-to-all-done.1, s32[1024]{0:T(1024)S(1)} %pad_clamp_fusion), kind=kCustom, calls=%fused_computation.1 | custom fusion | bytes 4194368 | tf_op jit(solution)/shard_map/gather | solution.py:118
  129.2 2.1 %multiply_reduce_fusion = f32[16,64]{1,0:T(8,128)S(1)} fusion(bf16[16,64,1024]{2,1,0:T(8,128)(2,1)} %gather_fusion.1), kind=kLoop, calls=%fused_computation.8 | loop fusion | flops 3144704 | bytes 2101248 | tf_op jit(solution)/shard_map/reduce_sum | solution.py:12
  131.4 2.1 %fusion = bf16[1024,1024]{1,0:T(8,128)(2,1)S(1)} fusion(f32[1024]{0:T(1024)S(1)} %rsqrt.33, bf16[16,64,1024]{2,1,0:T(8,128)(2,1)} %gather_fusion.1), kind=kLoop, calls=%fused_computation.3 | loop fusion | flops 3145728 | bytes 4198400 | tf_op jit(solution)/shard_map/convert_element_type | solution.py:12
  134.2 4.7 %convolution_convert_fusion = bf16[1024,2048]{1,0:T(8,128)(2,1)S(1)} fusion(bf16[1024,1024]{1,0:T(8,128)(2,1)S(1)} %fusion, bf16[1024,2048]{1,0:T(8,128)(2,1)S(1)} %copy-done.8), kind=kOutput, calls=%fused_computation.11 | convolution fusion | flops 4297064448 | bytes 10485760 | tf_op jit(solution)/shard_map/dot_general | solution.py:119
  138.9 2.6 %fusion.43 = (bf16[16,64,1024]{2,1,0:T(8,128)(2,1)}, bf16[16,64,1024]{2,1,0:T(8,128)(2,1)}) fusion(bf16[16,64,2048]{2,1,0:T(8,128)(2,1)S(1)} %bitcast.60), kind=kLoop, calls=%fused_computation.68 | loop fusion | bytes 8388608 | tf_op jit(solution)/shard_map/slice | solution.py:125
  141.5 6.4 %reshape.186 = bf16[16,64,16,64]{3,2,1,0:T(8,128)(2,1)} reshape(bf16[16,64,1024]{2,1,0:T(8,128)(2,1)} %get-tuple-element.5) | data formatting | bytes 4194304 | tf_op jit(solution)/shard_map/reshape | solution.py:125
  147.9 6.4 %reshape.185 = bf16[16,64,16,64]{3,2,1,0:T(8,128)(2,1)} reshape(bf16[16,64,1024]{2,1,0:T(8,128)(2,1)} %get-tuple-element.6) | data formatting | bytes 4194304 | tf_op jit(solution)/shard_map/reshape | solution.py:128
  154.3 4.7 %fusion.12 = (f32[16,16,16]{2,1,0:T(8,128)S(1)}, f32[16,16,16,64]{3,2,1,0:T(8,128)S(1)}) fusion(pred[16,64]{1,0:T(8,128)(4,1)S(1)} %iota_compare_fusion, bf16[16,64,16,64]{3,2,1,0:T(8,128)(2,1)} %reshape.186, bf16[16,16,16,64]{3,2,1,0:T(8,128)(2,1)S(1)} %reshape_reshape.3), kind=kOutput, calls=%fused_computation.21 | convolution fusion | flops 34336768 | bytes 3687424 | tf_op jit(solution)/shard_map/blhd,bkhd->bhlk/dot_general | solution.py:19
  159.0 1.3 fusion.15
  160.3 2.0 %fusion.9 = bf16[16,16,16,64]{3,1,2,0:T(8,128)(2,1)S(1)} fusion(bf16[16,64,16,64]{3,2,1,0:T(8,128)(2,1)S(1)} %copy-done.2, f32[16,16,16,64]{3,2,1,0:T(8,128)S(1)} %get-tuple-element.12, f32[16,16,16]{1,2,0:T(8,128)S(1)} %bitcast.65, f32[16,16,16]{2,1,0:T(8,128)S(1)} %get-tuple-element.11, pred[16,64]{1,0:T(8,128)(4,1)S(1)} %iota_compare_fusion), kind=kOutput, calls=%fused_computation.16 | convolution fusion | flops 35127296 | bytes 3703808 | tf_op jit(solution)/shard_map/bhlk,bkhd->blhd/dot_general | solution.py:27
  162.6 1.5 convert_element_type.85
  164.1 3.3 %fusion.20 = bf16[256,1024]{1,0:T(8,128)(2,1)} fusion(bf16[256,1024]{1,0:T(8,128)(2,1)} %convert_element_type.85, bf16[1024,1024]{1,0:T(8,128)(2,1)} %param.27, bf16[256,1024]{1,0:T(8,128)(2,1)} %copy-done.4), kind=kOutput, calls=%fused_computation.29 | convolution fusion | flops 537657344 | bytes 3670016 | tf_op jit(solution)/shard_map/dot_general | solution.py:137
  (39 shorter events, 3.2 us)
Async XLA Ops:
  0.0 120.5 %copy-start = (bf16[1024,1024]{1,0:T(8,128)(2,1)S(1)}, bf16[1024,1024]{1,0:T(8,128)(2,1)}, u32[]{:S(2)}) copy-start(bf16[1024,1024]{1,0:T(8,128)(2,1)} %param.24) | copy-start | bytes 6291460
  3.5 13.7 %all-to-all-start = ((s32[16,1,64]{2,1,0:T(1,128)}), s32[16,1,64]{2,1,0:T(1,128)S(1)}, u32[]{:S(2)}, u32[]{:S(2)}) async-start(s32[16,1,64]{2,1,0:T(1,128)} %bitcast.9), calls=%async_computation | async-start | bytes 16384 | tf_op jit(solution)/shard_map/all_to_all | solution.py:73
  24.7 4.7 %copy-start.1 = (bf16[16,16,1024]{2,1,0:T(8,128)(2,1)S(1)}, bf16[16,16,1024]{2,1,0:T(8,128)(2,1)}, u32[]{:S(2)}) copy-start(bf16[16,16,1024]{2,1,0:T(8,128)(2,1)} %param.14) | copy-start | bytes 1572868
  24.7 100.9 %all-to-all-start.1 = ((bf16[16,64,1024]{2,1,0:T(8,128)(2,1)}), bf16[16,64,1024]{2,1,0:T(8,128)(2,1)}, u32[]{:S(2)}, u32[]{:S(2)}) async-start(bf16[16,64,1024]{2,1,0:T(8,128)(2,1)} %bitcast.58), calls=%async_computation.1 | async-start | bytes 4194304 | tf_op jit(solution)/shard_map/all_to_all | solution.py:72
  29.5 4.4 %copy-start.5 = (bf16[16,1024]{1,0:T(8,128)(2,1)S(1)}, bf16[16,1024]{1,0:T(8,128)(2,1)}, u32[]{:S(2)}) copy-start(bf16[16,1024]{1,0:T(8,128)(2,1)} %param.21) | copy-start | bytes 98308
  32.7 56.2 %copy-start.6 = (bf16[16,1024]{1,0:T(8,128)(2,1)S(1)}, bf16[16,1024]{1,0:T(8,128)(2,1)}, u32[]{:S(2)}) copy-start(bf16[16,1024]{1,0:T(8,128)(2,1)} %param.22) | copy-start | bytes 98308
  118.6 1.0 copy-start.3
  120.5 1.7 %copy-start.9 = (bf16[1024,1024]{1,0:T(8,128)(2,1)S(1)}, bf16[1024,1024]{1,0:T(8,128)(2,1)}, u32[]{:S(2)}) copy-start(bf16[1024,1024]{1,0:T(8,128)(2,1)} %param.26) | copy-start | bytes 6291460
  121.4 0.8 copy-start.4
  122.2 3.4 %copy-start.7 = (s32[16]{0:T(128)S(1)}, s32[16]{0:T(128)}, u32[]{:S(2)}) copy-start(s32[16]{0:T(128)} %param.16) | copy-start | bytes 196
  131.4 2.8 %copy-start.8 = (bf16[1024,2048]{1,0:T(8,128)(2,1)S(1)}, bf16[1024,2048]{1,0:T(8,128)(2,1)}, u32[]{:S(2)}) copy-start(bf16[1024,2048]{1,0:T(8,128)(2,1)} %param.25) | copy-start | bytes 12582916
  154.3 6.1 %copy-start.2 = (bf16[16,64,16,64]{3,2,1,0:T(8,128)(2,1)S(1)}, bf16[16,64,16,64]{3,2,1,0:T(8,128)(2,1)}, u32[]{:S(2)}) copy-start(bf16[16,64,16,64]{3,2,1,0:T(8,128)(2,1)} %reshape.185) | copy-start | bytes 6291460
where the time goes:
time: 168 us; the launch traced here: 167 us
  blocking collectives  78.8 us (47%)
  local copies, waits for them, and re-layouts  37.3 us (22%)
  matrix products  22.9 us (14%)
  starting transfers between devices  11.9 us (7%)
  other arithmetic  11.2 us (7%)
  waiting for transfers between devices  5.11 us (3%)
    all_gather x1, blocking collectives, per_device(): lax.all_gather(memory_key, 'smp', axis=0, tiled=True)  52.9 us
    all_gather x1, blocking collectives, per_device(): lax.all_gather(memory_value, 'smp', axis=0, tiled=True)  25.8 us
    gather x1, local copies, waits for them, and re-layouts, per_device(): panel_table[lax.all_to_all(request, 'smp', split_axis=0, concat_axis=0, t...  7.42 us
    all_to_all x1, starting transfers between devices, per_device(): lax.all_to_all(request, 'smp', split_axis=0, concat_axis=0, tiled=True)  7.39 us
    reshape x1, local copies, waits for them, and re-layouts, per_device(): key_value[:, :, :model_width]  6.37 us
    reshape x1, local copies, waits for them, and re-layouts, per_device(): key_value[:, :, model_width:]  6.37 us
    all_to_all x1, waiting for transfers between devices, per_device(): lax.all_to_all(request, 'smp', split_axis=0, concat_axis=0, tiled=True)  5.11 us
    dot_general x1, matrix products, per_device(): jnp.dot(normed(embed.reshape(local_samples * token_total, model_width)),...  4.71 us
  transfers between devices with their start and end apart: 2, of which 1 were waited for; matrix products, arithmetic and copies ran while one was open for 10% of the time, Pallas kernels for 0%

commit v1 on v0

--- a/solution.py
+++ b/solution.py
@@ -5,6 +5,18 @@
 
 HEAD_DIM = 64
 masked_score = -1e30
+
+
+def gather_by_bits(x, axis, dim):
+    ways, here = (lax.axis_size(axis), lax.axis_index(axis))
+    grown, reach = (x, 1)
+    while reach < ways:
+        theirs = lax.ppermute(grown, axis, [(d, d ^ reach) for d in range(ways)])
+        mine_first = jnp.concatenate([grown, theirs], axis=dim)
+        theirs_first = jnp.concatenate([theirs, grown], axis=dim)
+        grown = jnp.where(here & reach == 0, mine_first, theirs_first)
+        reach = 2 * reach
+    return grown
 
 
 def normed(values):
@@ -86,9 +98,7 @@
     key_rows = lax.all_gather(memory_key, "smp", axis=0, tiled=True).reshape(
         -1, head_count, HEAD_DIM
     )
-    value_rows = lax.all_gather(memory_value, "smp", axis=0, tiled=True).reshape(
-        -1, head_count, HEAD_DIM
-    )
+    value_rows = gather_by_bits(memory_value, "smp", 0).reshape(-1, head_count, HEAD_DIM)
     scores = jnp.einsum(
         "rhd,khd->hrk", queries, key_rows, preferred_element_type=jnp.float32
     ) * HEAD_DIM ** (-0.5)

time: 168 us -> 177 us (1.054)
  blocking collectives: 78.8 us -> 57.4 us
  waiting for transfers between devices: 5.11 us -> 22.3 us
  starting transfers between devices: 11.9 us -> 23.6 us
  other arithmetic: 11.2 us -> 13.8 us
  local copies, waits for them, and re-layouts: 37.3 us -> 34.8 us
    all_gather x1 -> x0, blocking collectives: 25.8 us -> none  [per_device(): lax.all_gather(memory_value, 'smp', axis=0, tiled=True)]
    ppermute x0 -> x4, waiting for transfers between devices: none -> 22.3 us  [gather_by_bits(): theirs = lax.ppermute(grown, axis, [(d, d ^ reach) for d in range(ways)])]
    ppermute x0 -> x4, starting transfers between devices: none -> 10.5 us  [gather_by_bits(): theirs = lax.ppermute(grown, axis, [(d, d ^ reach) for d in range(ways)])]
    all_to_all x1, waiting for transfers between devices: 5.11 us -> 0.01 us  [per_device(): lax.all_to_all(request, 'smp', split_axis=0, concat_axis=0, tiled=True)]
    all_gather x1, blocking collectives: 52.9 us -> 57.4 us  [per_device(): lax.all_gather(memory_key, 'smp', axis=0, tiled=True)]
    dot_general x1, matrix products: 0.87 us -> 3.11 us  [per_device(): jnp.einsum('hrk,khd->hrd', exponent.astype(jnp.bfloat16), value_rows, pre...]
    gather x1, local copies, waits for them, and re-layouts: 7.42 us -> 5.37 us  [per_device(): panel_table[lax.all_to_all(request, 'smp', split_axis=0, concat_axis=0, t...]
    all_gather x1 -> x0, local copies, waits for them, and re-layouts: 2.04 us -> none  [per_device(): lax.all_gather(memory_value, 'smp', axis=0, tiled=True)]
  transfers between devices with their start and end apart: 2 -> 6, of which waited for: 1 -> 3; matrix products, arithmetic and copies ran while one was open for 10% -> 16% of each run, Pallas kernels for 0% -> 0%
where the time goes in v1:
time: 177 us; the launch traced here: 176 us
  blocking collectives  57.4 us (32%)
  local copies, waits for them, and re-layouts  34.8 us (20%)
  matrix products  24.2 us (14%)
  starting transfers between devices  23.6 us (13%)
  waiting for transfers between devices  22.3 us (13%)
  other arithmetic  13.8 us (8%)
    all_gather x1, blocking collectives, per_device(): lax.all_gather(memory_key, 'smp', axis=0, tiled=True)  57.4 us
    ppermute x4, waiting for transfers between devices, gather_by_bits(): theirs = lax.ppermute(grown, axis, [(d, d ^ reach) for d in range(ways)])  22.3 us
    ppermute x4, starting transfers between devices, gather_by_bits(): theirs = lax.ppermute(grown, axis, [(d, d ^ reach) for d in range(ways)])  10.5 us
    all_to_all x1, starting transfers between devices, per_device(): lax.all_to_all(request, 'smp', split_axis=0, concat_axis=0, tiled=True)  6.91 us
    reshape x1, local copies, waits for them, and re-layouts, per_device(): key_value[:, :, :model_width]  6.37 us
    reshape x1, local copies, waits for them, and re-layouts, per_device(): key_value[:, :, model_width:]  6.37 us
    all_to_all x1, starting transfers between devices, per_device(): lax.all_to_all(panel_table[lax.all_to_all(request, 'smp', split_axis=0, c...  6.19 us
    gather x1, local copies, waits for them, and re-layouts, per_device(): panel_table[lax.all_to_all(request, 'smp', split_axis=0, concat_axis=0, t...  5.37 us
  transfers between devices with their start and end apart: 6, of which 3 were waited for; matrix products, arithmetic and copies ran while one was open for 16% of the time, Pallas kernels for 0%

profile of v1, /device:TPU:0, one launch (start us, length us, event | category | flops | bytes accessed | tf_op | source)
XLA Modules:
  0.0 176.3 jit_solution(9231060530090173269)
XLA Ops:
  0.5 1.0 select_reduce_fusion.2
  4.0 6.9 %all-to-all-start = ((s32[16,1,64]{2,1,0:T(1,128)}), s32[16,1,64]{2,1,0:T(1,128)S(1)}, u32[]{:S(2)}, u32[]{:S(2)}) async-start(s32[16,1,64]{2,1,0:T(1,128)} %bitcast.13), calls=%async_computation | async-start | bytes 16384 | tf_op jit(solution)/shard_map/all_to_all | solution.py:85
  10.9 1.2 multiply_reduce_fusion.2
  12.2 1.2 fusion.31
  13.4 3.2 %convolution_convert_fusion.2 = bf16[256,1024]{1,0:T(8,128)(2,1)} fusion(bf16[256,1024]{1,0:T(8,128)(2,1)S(1)} %fusion.31, bf16[1024,1024]{1,0:T(8,128)(2,1)} %param.23), kind=kOutput, calls=%fused_computation.31 | convolution fusion | flops 537133056 | bytes 3145728 | tf_op jit(solution)/shard_map/dot_general | solution.py:93
  16.6 2.0 %copy.51 = bf16[256,1024]{0,1:T(8,128)(2,1)} copy(bf16[256,1024]{1,0:T(8,128)(2,1)} %convolution_convert_fusion.2) | data formatting | bytes 1048576 | tf_op jit(solution)/shard_map/convert_element_type | solution.py:93
  18.7 5.4 %gather_fusion = bf16[1024,1024]{1,0:T(8,128)(2,1)} fusion(bf16[512,1024]{1,0:T(8,128)(2,1)S(1)} %bitcast.60, s32[1024]{0:T(1024)S(1)} %broadcast_clamp_fusion), kind=kCustom, calls=%fused_computation | custom fusion | bytes 4198400 | tf_op jit(solution)/shard_map/gather | solution.py:85
  24.1 6.2 %all-to-all-start.1 = ((bf16[16,64,1024]{2,1,0:T(8,128)(2,1)}), bf16[16,64,1024]{2,1,0:T(8,128)(2,1)}, u32[]{:S(2)}, u32[]{:S(2)}) async-start(bf16[16,64,1024]{2,1,0:T(8,128)(2,1)} %bitcast.61), calls=%async_computation.1 | async-start | bytes 4194304 | tf_op jit(solution)/shard_map/all_to_all | solution.py:84
  30.3 57.4 %all_gather.3 = bf16[256,1024]{1,0:T(8,128)(2,1)} all-gather(bf16[16,1024]{1,0:T(8,128)(2,1)S(1)} %copy-done.8), channel_id=1, replica_groups=mesh['grp'=2,'smp'=16] {'smp'}, dimensions={0}, use_global_device_ids=true | all-gather | bytes 557056 | tf_op jit(solution)/shard_map/all_gather | solution.py:98
  87.7 1.2 copy.52
  90.5 1.2 copy-done.2
  92.0 3.1 %collective-permute-start.1 = (bf16[32,1024]{0,1:T(8,128)(2,1)S(1)}, bf16[32,1024]{0,1:T(8,128)(2,1)S(1)}, u32[]{:S(2)}, u32[]{:S(2)}) collective-permute-start(bf16[32,1024]{0,1:T(8,128)(2,1)S(1)} %broadcast_select_fusion), channel_id=1, source_target_pairs={{0,2},{1,3},{2,0},{3,1},{4,6},{5,7},{6,4},{7,5},{8,10},{9,11},{10,... | collective-permute-start | bytes 196616 | tf_op jit(solution)/shard_map/ppermute | solution.py:14
  95.2 6.6 %collective-permute-done.1 = bf16[32,1024]{0,1:T(8,128)(2,1)S(1)} collective-permute-done((bf16[32,1024]{0,1:T(8,128)(2,1)S(1)}, bf16[32,1024]{0,1:T(8,128)(2,1)S(1)}, u32[]{:S(2)}, u32[]{:S(2)}) %collective-permute-start.1) | collective-permute-done | bytes 65568 | tf_op jit(solution)/shard_map/ppermute | solution.py:14
  102.1 4.2 %collective-permute-start.2 = (bf16[64,1024]{0,1:T(8,128)(2,1)S(1)}, bf16[64,1024]{0,1:T(8,128)(2,1)S(1)}, u32[]{:S(2)}, u32[]{:S(2)}) collective-permute-start(bf16[64,1024]{0,1:T(8,128)(2,1)S(1)} %maximum_select_fusion.4), channel_id=1, source_target_pairs={{0,4},{1,5},{2,6},{3,7},{4,0},{5,1},{6,2},{7,3},{8,12},{9,13},{10,... | collective-permute-start | bytes 393224 | tf_op jit(solution)/shard_map/ppermute | solution.py:14
  106.7 5.6 %collective-permute-done.2 = bf16[64,1024]{0,1:T(8,128)(2,1)S(1)} collective-permute-done((bf16[64,1024]{0,1:T(8,128)(2,1)S(1)}, bf16[64,1024]{0,1:T(8,128)(2,1)S(1)}, u32[]{:S(2)}, u32[]{:S(2)}) %collective-permute-start.2) | collective-permute-done | bytes 131104 | tf_op jit(solution)/shard_map/ppermute | solution.py:14
  112.6 2.7 %collective-permute-start.3 = (bf16[128,1024]{0,1:T(8,128)(2,1)S(1)}, bf16[128,1024]{0,1:T(8,128)(2,1)S(1)}, u32[]{:S(2)}, u32[]{:S(2)}) collective-permute-start(bf16[128,1024]{0,1:T(8,128)(2,1)S(1)} %maximum_select_fusion.6), channel_id=1, source_target_pairs={{0,8},{1,9},{2,10},{3,11},{4,12},{5,13},{6,14},{7,15},{8,0},{9,1},... | collective-permute-start | bytes 786440 | tf_op jit(solution)/shard_map/ppermute | solution.py:14
  116.2 10.1 %collective-permute-done.3 = bf16[128,1024]{0,1:T(8,128)(2,1)S(1)} collective-permute-done((bf16[128,1024]{0,1:T(8,128)(2,1)S(1)}, bf16[128,1024]{0,1:T(8,128)(2,1)S(1)}, u32[]{:S(2)}, u32[]{:S(2)}) %collective-permute-start.3) | collective-permute-done | bytes 262176 | tf_op jit(solution)/shard_map/ppermute | solution.py:14
  126.3 3.1 %fusion.25 = bf16[256,16,64]{0,2,1:T(8,128)(2,1)S(1)} fusion(f32[16,256,256]{1,2,0:T(8,128)} %copy-done.2, f32[16,256]{1,0:T(8,128)S(1)} %broadcast_maximum_fusion, bf16[128,16,64]{0,2,1:T(8,128)(2,1)S(1)} %bitcast.74, bf16[128,16,64]{0,2,1:T(8,128)(2,1)S(1)} %maximum_select_fusion.5, f32[256,16]{0,1:T(8,128)S(1)} %bitcast.73, pred[]{:T(512)S(6)} %eq.69), kind=kOutput, calls=%fused_computation.34 | convolution fusion | flops 140247040 | bytes 5275649 | tf_op jit(solution)/shard_map/hrk,khd->hrd/dot_general | solution.py:108
  131.2 1.6 convolution_convert_fusion.1
  132.7 1.8 reshape_reshape.3
  134.5 3.6 %gather_fusion.1 = bf16[16,64,1024]{2,1,0:T(8,128)(2,1)} fusion(bf16[16,64,1024]{2,1,0:T(8,128)(2,1)} %all-to-all-done.1, s32[1024]{0:T(1024)S(1)} %pad_clamp_fusion), kind=kCustom, calls=%fused_computation.1 | custom fusion | bytes 4194368 | tf_op jit(solution)/shard_map/gather | solution.py:128
  138.1 2.1 %multiply_reduce_fusion = f32[16,64]{1,0:T(8,128)S(1)} fusion(bf16[16,64,1024]{2,1,0:T(8,128)(2,1)} %gather_fusion.1), kind=kLoop, calls=%fused_computation.8 | loop fusion | flops 3144704 | bytes 2101248 | tf_op jit(solution)/shard_map/reduce_sum | solution.py:24
  140.3 2.1 %fusion = bf16[1024,1024]{1,0:T(8,128)(2,1)S(1)} fusion(f32[1024]{0:T(1024)S(1)} %rsqrt.33, bf16[16,64,1024]{2,1,0:T(8,128)(2,1)} %gather_fusion.1), kind=kLoop, calls=%fused_computation.3 | loop fusion | flops 3145728 | bytes 4198400 | tf_op jit(solution)/shard_map/convert_element_type | solution.py:24
  143.1 4.7 %convolution_convert_fusion = bf16[1024,2048]{1,0:T(8,128)(2,1)S(1)} fusion(bf16[1024,1024]{1,0:T(8,128)(2,1)S(1)} %fusion, bf16[1024,2048]{1,0:T(8,128)(2,1)S(1)} %copy-done.10), kind=kOutput, calls=%fused_computation.11 | convolution fusion | flops 4297064448 | bytes 10485760 | tf_op jit(solution)/shard_map/dot_general | solution.py:129
  147.8 2.6 %fusion.50 = (bf16[16,64,1024]{2,1,0:T(8,128)(2,1)}, bf16[16,64,1024]{2,1,0:T(8,128)(2,1)}) fusion(bf16[16,64,2048]{2,1,0:T(8,128)(2,1)S(1)} %bitcast.63), kind=kLoop, calls=%fused_computation.84 | loop fusion | bytes 8388608 | tf_op jit(solution)/shard_map/slice | solution.py:135
  150.4 6.4 %reshape.199 = bf16[16,64,16,64]{3,2,1,0:T(8,128)(2,1)} reshape(bf16[16,64,1024]{2,1,0:T(8,128)(2,1)} %get-tuple-element.5) | data formatting | bytes 4194304 | tf_op jit(solution)/shard_map/reshape | solution.py:135
  156.8 6.4 %reshape.198 = bf16[16,64,16,64]{3,2,1,0:T(8,128)(2,1)} reshape(bf16[16,64,1024]{2,1,0:T(8,128)(2,1)} %get-tuple-element.6) | data formatting | bytes 4194304 | tf_op jit(solution)/shard_map/reshape | solution.py:138
  163.2 4.7 %fusion.12 = (f32[16,16,16]{2,1,0:T(8,128)S(1)}, f32[16,16,16,64]{3,2,1,0:T(8,128)S(1)}) fusion(pred[16,64]{1,0:T(8,128)(4,1)S(1)} %iota_compare_fusion, bf16[16,64,16,64]{3,2,1,0:T(8,128)(2,1)} %reshape.199, bf16[16,16,16,64]{3,2,1,0:T(8,128)(2,1)S(1)} %reshape_reshape.3), kind=kOutput, calls=%fused_computation.21 | convolution fusion | flops 34336768 | bytes 3687424 | tf_op jit(solution)/shard_map/blhd,bkhd->bhlk/dot_general | solution.py:31
  167.9 1.3 fusion.15
  169.2 2.0 %fusion.9 = bf16[16,16,16,64]{3,1,2,0:T(8,128)(2,1)S(1)} fusion(bf16[16,64,16,64]{3,2,1,0:T(8,128)(2,1)S(1)} %copy-done.4, f32[16,16,16,64]{3,2,1,0:T(8,128)S(1)} %get-tuple-element.14, f32[16,16,16]{1,2,0:T(8,128)S(1)} %bitcast.71, f32[16,16,16]{2,1,0:T(8,128)S(1)} %get-tuple-element.13, pred[16,64]{1,0:T(8,128)(4,1)S(1)} %iota_compare_fusion), kind=kOutput, calls=%fused_computation.16 | convolution fusion | flops 35127296 | bytes 3703808 | tf_op jit(solution)/shard_map/bhlk,bkhd->blhd/dot_general | solution.py:39
  171.5 1.5 convert_element_type.85
  173.0 3.3 %fusion.20 = bf16[256,1024]{1,0:T(8,128)(2,1)} fusion(bf16[256,1024]{1,0:T(8,128)(2,1)} %convert_element_type.85, bf16[1024,1024]{1,0:T(8,128)(2,1)} %param.27, bf16[256,1024]{1,0:T(8,128)(2,1)} %copy-done.6), kind=kOutput, calls=%fused_computation.29 | convolution fusion | flops 537657344 | bytes 3670016 | tf_op jit(solution)/shard_map/dot_general | solution.py:147
  (60 shorter events, 9.6 us)
Async XLA Ops:
  0.0 129.5 %copy-start = (bf16[1024,1024]{1,0:T(8,128)(2,1)S(1)}, bf16[1024,1024]{1,0:T(8,128)(2,1)}, u32[]{:S(2)}) copy-start(bf16[1024,1024]{1,0:T(8,128)(2,1)} %param.24) | copy-start | bytes 6291460
  0.0 91.6 %collective-permute-start = (bf16[16,1024]{1,0:T(8,128)(2,1)}, bf16[16,1024]{1,0:T(8,128)(2,1)S(1)}, u32[]{:S(2)}, u32[]{:S(2)}) collective-permute-start(bf16[16,1024]{1,0:T(8,128)(2,1)} %param.22), channel_id=1, source_target_pairs={{0,1},{1,0},{2,3},{3,2},{4,5},{5,4},{6,7},{7,6},{8,9},{9,8},{10,11... | collective-permute-start | bytes 98312 | tf_op jit(solution)/shard_map/ppermute | solution.py:14
  4.0 14.7 %all-to-all-start = ((s32[16,1,64]{2,1,0:T(1,128)}), s32[16,1,64]{2,1,0:T(1,128)S(1)}, u32[]{:S(2)}, u32[]{:S(2)}) async-start(s32[16,1,64]{2,1,0:T(1,128)} %bitcast.13), calls=%async_computation | async-start | bytes 16384 | tf_op jit(solution)/shard_map/all_to_all | solution.py:85
  13.4 5.3 %copy-start.1 = (bf16[1,512,1024]{2,1,0:T(8,128)(2,1)S(1)}, bf16[1,512,1024]{2,1,0:T(8,128)(2,1)}, u32[]{:S(2)}) copy-start(bf16[1,512,1024]{2,1,0:T(8,128)(2,1)} %param.20) | copy-start | bytes 3145732
  24.1 6.2 %copy-start.8 = (bf16[16,1024]{1,0:T(8,128)(2,1)S(1)}, bf16[16,1024]{1,0:T(8,128)(2,1)}, u32[]{:S(2)}) copy-start(bf16[16,1024]{1,0:T(8,128)(2,1)} %param.21) | copy-start | bytes 98308
  24.1 64.8 %copy-start.5 = (bf16[256,1024]{0,1:T(8,128)(2,1)S(1)}, bf16[256,1024]{0,1:T(8,128)(2,1)}, u32[]{:S(2)}) copy-start(bf16[256,1024]{0,1:T(8,128)(2,1)} %copy.51) | copy-start | bytes 1572868
  24.1 110.4 %all-to-all-start.1 = ((bf16[16,64,1024]{2,1,0:T(8,128)(2,1)}), bf16[16,64,1024]{2,1,0:T(8,128)(2,1)}, u32[]{:S(2)}, u32[]{:S(2)}) async-start(bf16[16,64,1024]{2,1,0:T(8,128)(2,1)} %bitcast.61), calls=%async_computation.1 | async-start | bytes 4194304 | tf_op jit(solution)/shard_map/all_to_all | solution.py:84
  89.7 1.9 %copy-start.2 = (f32[16,256,256]{1,2,0:T(8,128)}, f32[16,256,256]{1,2,0:T(8,128)S(1)}, u32[]{:S(2)}) copy-start(f32[16,256,256]{1,2,0:T(8,128)S(1)} %get-tuple-element.10) | copy-start | bytes 12582916
  89.7 1.9 %copy-start.7 = (bf16[16,1024]{1,0:T(8,128)(2,1)S(1)}, bf16[16,1024]{1,0:T(8,128)(2,1)}, u32[]{:S(2)}) copy-start(bf16[16,1024]{1,0:T(8,128)(2,1)} %param.22) | copy-start | bytes 98308
  89.7 5.4 %copy-start.9 = (s32[16]{0:T(128)S(1)}, s32[16]{0:T(128)}, u32[]{:S(2)}) copy-start(s32[16]{0:T(128)} %param.16) | copy-start | bytes 196
  92.0 9.7 %collective-permute-start.1 = (bf16[32,1024]{0,1:T(8,128)(2,1)S(1)}, bf16[32,1024]{0,1:T(8,128)(2,1)S(1)}, u32[]{:S(2)}, u32[]{:S(2)}) collective-permute-start(bf16[32,1024]{0,1:T(8,128)(2,1)S(1)} %broadcast_select_fusion), channel_id=1, source_target_pairs={{0,2},{1,3},{2,0},{3,1},{4,6},{5,7},{6,4},{7,5},{8,10},{9,11},{10,... | collective-permute-start | bytes 196616 | tf_op jit(solution)/shard_map/ppermute | solution.py:14
  102.1 10.2 %collective-permute-start.2 = (bf16[64,1024]{0,1:T(8,128)(2,1)S(1)}, bf16[64,1024]{0,1:T(8,128)(2,1)S(1)}, u32[]{:S(2)}, u32[]{:S(2)}) collective-permute-start(bf16[64,1024]{0,1:T(8,128)(2,1)S(1)} %maximum_select_fusion.4), channel_id=1, source_target_pairs={{0,4},{1,5},{2,6},{3,7},{4,0},{5,1},{6,2},{7,3},{8,12},{9,13},{10,... | collective-permute-start | bytes 393224 | tf_op jit(solution)/shard_map/ppermute | solution.py:14
  112.6 13.7 %collective-permute-start.3 = (bf16[128,1024]{0,1:T(8,128)(2,1)S(1)}, bf16[128,1024]{0,1:T(8,128)(2,1)S(1)}, u32[]{:S(2)}, u32[]{:S(2)}) collective-permute-start(bf16[128,1024]{0,1:T(8,128)(2,1)S(1)} %maximum_select_fusion.6), channel_id=1, source_target_pairs={{0,8},{1,9},{2,10},{3,11},{4,12},{5,13},{6,14},{7,15},{8,0},{9,1},... | collective-permute-start | bytes 786440 | tf_op jit(solution)/shard_map/ppermute | solution.py:14
  126.3 3.1 %copy-start.3 = (bf16[16,16,1024]{2,1,0:T(8,128)(2,1)S(1)}, bf16[16,16,1024]{2,1,0:T(8,128)(2,1)}, u32[]{:S(2)}) copy-start(bf16[16,16,1024]{2,1,0:T(8,128)(2,1)} %param.14) | copy-start | bytes 1572868
  129.5 1.7 copy-start.11
  130.3 0.8 copy-start.6
  140.3 2.8 %copy-start.10 = (bf16[1024,2048]{1,0:T(8,128)(2,1)S(1)}, bf16[1024,2048]{1,0:T(8,128)(2,1)}, u32[]{:S(2)}) copy-start(bf16[1024,2048]{1,0:T(8,128)(2,1)} %param.25) | copy-start | bytes 12582916
  163.2 6.1 %copy-start.4 = (bf16[16,64,16,64]{3,2,1,0:T(8,128)(2,1)S(1)}, bf16[16,64,16,64]{3,2,1,0:T(8,128)(2,1)}, u32[]{:S(2)}) copy-start(bf16[16,64,16,64]{3,2,1,0:T(8,128)(2,1)} %reshape.198) | copy-start | bytes 6291460
